TPU v7x, 512 devices: a whole 4x8x8 slice. The times are simulated.
512 devices in a mesh: row: 32 (over y, x), col: 16 (over z, core).
Axes of the slice: x: 4, y: 8, z: 8, core: 2. Of those that a mesh axis runs over, the one named last changes fastest.
Arguments:
- stored: float32 [8192, 8192], P('row', 'col'), as said below
Outputs:
- factored: float32 [8192, 8192], P('row', 'col')
Inputs may be any that keep to these rules, and one draw needn't show every extreme that they name: stored is the storage order of a symmetric positive definite matrix.
All inputs are finite; a program needn't handle non-finite values.
Results may differ from a plain program's by a relative error of at most 0.0001.
Values sent between devices are 32-bit elements; how exact they have to be, the bound alone decides.
No kernel may reach another device: no remote copies, remote signals or barrier semaphores. Data moves between devices by JAX's collectives and lax.ppermute only.
A program may use at most 64 MiB of HBM per device.

v0:
```python
import jax
import jax.numpy as jnp
from jax import lax
from jax.sharding import PartitionSpec as P

NB = 64


def spread(array, axis, root):
    mine = lax.axis_index(axis) == root
    return lax.psum(jnp.where(mine, array, jnp.zeros_like(array)), axis)


def factor_panel(matrix, panel_index, row_ids, nrows, ncols):
    local_col = panel_index // ncols
    local_row = panel_index // nrows
    corner = matrix[local_row * NB : (local_row + 1) * NB, local_col * NB : (local_col + 1) * NB]
    corner = spread(corner, "row", panel_index % nrows)
    diag_factor = jnp.linalg.cholesky(corner)
    column_part = matrix[:, local_col * NB : (local_col + 1) * NB]
    solved = jax.scipy.linalg.solve_triangular(diag_factor, column_part.T, lower=True).T
    column_local = jnp.where(row_ids[:, None] > panel_index, solved, 0.0)
    current = column_local[local_row * NB : (local_row + 1) * NB]
    is_diag = row_ids[local_row * NB] == panel_index
    column_local = column_local.at[local_row * NB : (local_row + 1) * NB].set(
        jnp.where(is_diag, diag_factor, current)
    )
    return spread(column_local, "col", panel_index % ncols)


def matching_rows(panel_block, col_pos, nrows, ncols, row_count, col_count):
    gathered = lax.all_gather(panel_block, "row", axis=0, tiled=True)
    ordered = (
        gathered.reshape(nrows, row_count, NB, NB)
        .transpose(1, 0, 2, 3)
        .reshape(nrows * row_count, NB, NB)
    )
    wanted = jnp.arange(col_count, dtype=jnp.int32) * ncols + col_pos
    picked = jnp.take(ordered, wanted, axis=0)
    return picked.reshape(col_count * NB, NB)


def trailing_update(matrix, panel_block, picked, panel_index, row_ids, col_ids):
    product = jnp.dot(
        panel_block, picked.T, precision=lax.Precision.HIGHEST, preferred_element_type=jnp.float32
    )
    keep_cells = (row_ids[:, None] > panel_index) & (col_ids[None, :] > panel_index) & True
    return matrix - jnp.where(keep_cells, product, 0.0)


def set_column(matrix, panel_block, panel_index, col_pos, ncols):
    local_col = panel_index // ncols
    current = matrix[:, local_col * NB : (local_col + 1) * NB]
    return matrix.at[:, local_col * NB : (local_col + 1) * NB].set(
        jnp.where(col_pos == panel_index % ncols, panel_block, current)
    )


def per_device(stored):
    nrows = lax.axis_size("row")
    ncols = lax.axis_size("col")
    row_pos = lax.axis_index("row")
    col_pos = lax.axis_index("col")
    row_count = stored.shape[0] // NB
    col_count = stored.shape[1] // NB
    row_ids = jnp.arange(row_count * NB, dtype=jnp.int32) // NB * nrows + row_pos
    col_ids = jnp.arange(col_count * NB, dtype=jnp.int32) // NB * ncols + col_pos
    matrix = stored
    for panel_index in range(2):
        panel_block = factor_panel(matrix, panel_index, row_ids, nrows, ncols)
        picked = matching_rows(panel_block, col_pos, nrows, ncols, row_count, col_count)
        matrix = trailing_update(matrix, panel_block, picked, panel_index, row_ids, col_ids)
        matrix = set_column(matrix, panel_block, panel_index, col_pos, ncols)
    upper = (col_ids[None, :] >= 2) & (row_ids[:, None] < col_ids[None, :])
    return jnp.where(upper, 0.0, matrix)


def solution(mesh):
    return jax.shard_map(
        per_device,
        mesh=mesh,
        in_specs=(P("row", "col"),),
        out_specs=P("row", "col"),
        check_vma=False,
    )
```

profile of v0, /device:TPU:8, one launch (start us, length us, event | category | flops | bytes accessed | tf_op | source)
XLA Modules:
  0.0 751.8 jit_solution(203462624327193915)
XLA Ops:
  6.6 0.8 slice_select_fusion.3
  7.3 137.1 %psum.28 = f32[64,64]{1,0:T(8,128)S(1)} all-reduce(f32[64,64]{1,0:T(8,128)S(1)} %slice_select_fusion.3), channel_id=1, replica_groups=mesh['row'=32,'col'=16] {'row'}, use_global_device_ids=true, to_apply=%region_0.1 | all-reduce | flops 4096 | bytes 32768 | tf_op jit(solution)/shard_map/psum | solution.py:11
  144.6 5.9 cholesky.44
  150.5 0.6 compare_reduce_fusion.1
  151.2 0.7 select_bitcast_fusion.1
  151.8 4.9 custom-call.6
  157.3 1.2 fusion.3
  159.2 0.7 fusion.8
  159.8 0.7 broadcast_select_fusion.3
  160.6 119.0 %all-reduce.3.cloned.1.call-done = f32[256,64]{1,0:T(8,128)} async-done(((f32[256,64]{1,0:T(8,128)}), f32[256,64]{1,0:T(8,128)}) %all-reduce.3.cloned.1.call-update) | async-done | bytes 65552 | tf_op jit(solution)/shard_map/psum | solution.py:11
  280.3 0.7 compare_reduce_fusion.2
  281.1 89.3 %all-gather.3.cloned.1.call-done = f32[8192,64]{1,0:T(8,128)} async-done(((f32[256,64]{1,0:T(8,128)}), f32[8192,64]{1,0:T(8,128)}) %all-gather.3.cloned.1.call-update) | async-done | bytes 2097168 | tf_op jit(solution)/shard_map/all_gather | solution.py:32
  370.4 4.8 copy.11
  375.2 2.7 gather_fusion
  378.1 0.6 fusion
  378.7 0.7 select_select_fusion.1
  379.4 134.2 %psum.30 = f32[64,64]{1,0:T(8,128)S(1)} all-reduce(f32[64,64]{1,0:T(8,128)S(1)} %slice_select_fusion.1), channel_id=1, replica_groups=mesh['row'=32,'col'=16] {'row'}, use_global_device_ids=true, to_apply=%region_5.9 | all-reduce | flops 4096 | bytes 32768 | tf_op jit(solution)/shard_map/psum | solution.py:11
  513.7 5.9 cholesky.55
  519.6 0.6 compare_reduce_fusion
  520.3 0.7 select_bitcast_fusion
  520.9 4.9 custom-call.7
  526.1 0.7 fusion.7
  526.8 0.7 broadcast_select_fusion.2
  527.5 116.5 %all-reduce.5.cloned.1.call-done = f32[256,64]{1,0:T(8,128)} async-done(((f32[256,64]{1,0:T(8,128)}), f32[256,64]{1,0:T(8,128)}) %all-reduce.5.cloned.1.call-update) | async-done | bytes 65552 | tf_op jit(solution)/shard_map/psum | solution.py:11
  644.1 1.1 scatter.15
  645.2 89.1 %all-gather.5.cloned.1.call-done = f32[8192,64]{1,0:T(8,128)} async-done(((f32[256,64]{1,0:T(8,128)}), f32[8192,64]{1,0:T(8,128)}) %all-gather.5.cloned.1.call-update) | async-done | bytes 2097168 | tf_op jit(solution)/shard_map/all_gather | solution.py:32
  734.2 4.8 copy.15
  739.0 2.7 gather_fusion.1
  741.9 0.6 fusion.1
  742.5 0.7 select_select_fusion
  743.2 1.1 scatter.19
  744.3 0.9 and_select_fusion
  (36 shorter events, 1.7 us)
Async XLA Ops:
  6.5 273.0 %all-reduce.3.cloned.1.call-start = ((), (), s32[]{:S(2)}) async-start(), calls=%async_computation | async-start | bytes 262144 | tf_op jit(solution)/shard_map/psum | solution.py:11
  160.5 209.8 %all-gather.3.cloned.1.call-start = ((), (), s32[]{:S(2)}) async-start(), calls=%async_computation.1 | async-start | bytes 4325376 | tf_op jit(solution)/shard_map/all_gather | solution.py:32
  279.6 364.5 %all-reduce.5.cloned.1.call-start = ((), (), s32[]{:S(2)}) async-start(), calls=%async_computation.2 | async-start | bytes 262144 | tf_op jit(solution)/shard_map/psum | solution.py:11
  370.4 7.7 %copy-start = (f32[256,64]{1,0:T(8,128)S(1)}, f32[256,64]{1,0:T(8,128)}, u32[]{:S(2)}) copy-start(f32[256,64]{1,0:T(8,128)} %all-reduce.3.cloned.1.call-done) | copy-start | bytes 196612
  370.4 7.7 %copy-start.2 = (f32[256,512]{1,0:T(8,128)S(1)}, f32[256,512]{1,0:T(8,128)}, u32[]{:S(2)}) copy-start(f32[256,512]{1,0:T(8,128)} %param.14) | copy-start | bytes 1572868
  527.5 206.7 %all-gather.5.cloned.1.call-start = ((), (), s32[]{:S(2)}) async-start(), calls=%async_computation.3 | async-start | bytes 4325376 | tf_op jit(solution)/shard_map/all_gather | solution.py:32
  734.2 7.6 %copy-start.1 = (f32[256,64]{1,0:T(8,128)S(1)}, f32[256,64]{1,0:T(8,128)}, u32[]{:S(2)}) copy-start(f32[256,64]{1,0:T(8,128)} %all-reduce.5.cloned.1.call-done) | copy-start | bytes 196612
Sparse Core Ops, SparseCore 0:
  160.6 118.8 all-reduce.2
  283.2 87.1 all-gather.2
  527.6 116.3 all-reduce.4
  647.1 87.1 all-gather.4
where the time goes:
time: 752 us
  waiting for transfers between devices  414 us (55%)
  blocking collectives  271 us (36%)
  other arithmetic  30.9 us (4%)
  local copies, waits for them, and re-layouts  18.1 us (2%)
  between operations  14.7 us (2%)
    psum x2, blocking collectives, spread(): return lax.psum(jnp.where(mine, array, jnp.zeros_like(array)), axis)  271 us
    psum x2, waiting for transfers between devices, spread(): return lax.psum(jnp.where(mine, array, jnp.zeros_like(array)), axis)  235 us
    all_gather x2, waiting for transfers between devices, matching_rows(): gathered = lax.all_gather(panel_block, 'row', axis=0, tiled=True)  178 us
  transfers between devices with their start and end apart: 4, of which 4 were waited for; matrix products, arithmetic and copies ran while one was open for 0% of the time, Pallas kernels for 0%

commit v1 on v0

--- a/solution.py
+++ b/solution.py
@@ -29,7 +29,9 @@
 
 
 def matching_rows(panel_block, col_pos, nrows, ncols, row_count, col_count):
-    gathered = lax.all_gather(panel_block, "row", axis=0, tiled=True)
+    gathered = jnp.concatenate(
+        lax.all_to_all(jnp.stack([panel_block] * lax.axis_size("row")), "row", 0, 0), axis=0
+    )
     ordered = (
         gathered.reshape(nrows, row_count, NB, NB)
         .transpose(1, 0, 2, 3)

time: 752 us -> 701 us (0.932)
  the two profiles are of different devices: /device:TPU:8 before, /device:TPU:16 now
where the time goes in v1:
time: 701 us; the launch traced here: 700 us
  waiting for transfers between devices  343 us (49%)
  blocking collectives  259 us (37%)
  other arithmetic  30.9 us (4%)
  local copies, waits for them, and re-layouts  30.4 us (4%)
  starting transfers between devices  19.7 us (3%)
  between operations  15 us (2%)
    psum x2, blocking collectives, spread(): return lax.psum(jnp.where(mine, array, jnp.zeros_like(array)), axis)  259 us
    psum x2, waiting for transfers between devices, spread(): return lax.psum(jnp.where(mine, array, jnp.zeros_like(array)), axis)  245 us
    all_to_all x2, waiting for transfers between devices, matching_rows(): lax.all_to_all(jnp.stack([panel_block] * lax.axis_size('row')), 'row', 0, 0)  98 us
    all_to_all x2, starting transfers between devices, matching_rows(): lax.all_to_all(jnp.stack([panel_block] * lax.axis_size('row')), 'row', 0, 0)  19.7 us
  transfers between devices with their start and end apart: 4, of which 4 were waited for; matrix products, arithmetic and copies ran while one was open for 0% of the time, Pallas kernels for 0%

profile of v1, /device:TPU:16, one launch (start us, length us, event | category | flops | bytes accessed | tf_op | source)
XLA Modules:
  0.0 700.0 jit_solution(16093616118656020360)
XLA Ops:
  6.6 0.8 slice_select_fusion.3
  7.3 131.0 %psum.28 = f32[64,64]{1,0:T(8,128)S(1)} all-reduce(f32[64,64]{1,0:T(8,128)S(1)} %slice_select_fusion.3), channel_id=1, replica_groups=mesh['row'=32,'col'=16] {'row'}, use_global_device_ids=true, to_apply=%region_0.1 | all-reduce | flops 4096 | bytes 32768 | tf_op jit(solution)/shard_map/psum | solution.py:11
  138.5 5.9 cholesky.44
  145.7 4.9 custom-call.6
  151.2 1.2 fusion.3
  153.7 0.7 broadcast_select_fusion.3
  154.4 125.1 %all-reduce.3.cloned.1.call-done = f32[256,64]{1,0:T(8,128)} async-done(((f32[256,64]{1,0:T(8,128)}), f32[256,64]{1,0:T(8,128)}) %all-reduce.3.cloned.1.call-update) | async-done | bytes 65552 | tf_op jit(solution)/shard_map/psum | solution.py:11
  279.5 1.0 copy.17
  280.5 1.6 stack.4
  282.0 9.8 %all-to-all-start = ((f32[32,256,64]{1,2,0:T(8,128)}), f32[32,256,64]{1,2,0:T(8,128)S(1)}, u32[]{:S(2)}, u32[]{:S(2)}) async-start(f32[32,256,64]{1,2,0:T(8,128)} %stack.4), calls=%async_computation | async-start | bytes 4194304 | tf_op jit(solution)/shard_map/all_to_all | solution.py:33
  292.6 0.7 compare_reduce_fusion.2
  293.4 48.8 %all-to-all-done = f32[32,256,64]{1,2,0:T(8,128)S(1)} async-done(((f32[32,256,64]{1,2,0:T(8,128)}), f32[32,256,64]{1,2,0:T(8,128)S(1)}, u32[]{:S(2)}, u32[]{:S(2)}) %all-to-all-start) | async-done | bytes 2097184 | tf_op jit(solution)/shard_map/all_to_all | solution.py:33
  342.2 3.1 reshape_reshape.6
  345.2 5.3 copy.18
  350.5 2.7 gather_fusion
  354.0 0.7 select_select_fusion.1
  354.8 127.6 %psum.30 = f32[64,64]{1,0:T(8,128)S(1)} all-reduce(f32[64,64]{1,0:T(8,128)S(1)} %slice_select_fusion.1), channel_id=1, replica_groups=mesh['row'=32,'col'=16] {'row'}, use_global_device_ids=true, to_apply=%region_5.9 | all-reduce | flops 4096 | bytes 32768 | tf_op jit(solution)/shard_map/psum | solution.py:11
  482.5 5.9 cholesky.55
  489.7 4.9 custom-call.7
  495.5 0.7 broadcast_select_fusion.2
  496.2 119.7 %all-reduce.5.cloned.1.call-done = f32[256,64]{1,0:T(8,128)} async-done(((f32[256,64]{1,0:T(8,128)}), f32[256,64]{1,0:T(8,128)}) %all-reduce.5.cloned.1.call-update) | async-done | bytes 65552 | tf_op jit(solution)/shard_map/psum | solution.py:11
  615.9 1.0 copy.22
  616.9 1.6 stack.5
  618.5 9.8 %all-to-all-start.1 = ((f32[32,256,64]{1,2,0:T(8,128)}), f32[32,256,64]{1,2,0:T(8,128)S(1)}, u32[]{:S(2)}, u32[]{:S(2)}) async-start(f32[32,256,64]{1,2,0:T(8,128)} %stack.5), calls=%async_computation.1 | async-start | bytes 4194304 | tf_op jit(solution)/shard_map/all_to_all | solution.py:33
  628.4 1.1 scatter.15
  629.4 49.2 %all-to-all-done.1 = f32[32,256,64]{1,2,0:T(8,128)S(1)} async-done(((f32[32,256,64]{1,2,0:T(8,128)}), f32[32,256,64]{1,2,0:T(8,128)S(1)}, u32[]{:S(2)}, u32[]{:S(2)}) %all-to-all-start.1) | async-done | bytes 2097184 | tf_op jit(solution)/shard_map/all_to_all | solution.py:33
  678.6 3.1 reshape_reshape.7
  681.7 5.3 copy.23
  687.0 2.7 gather_fusion.1
  690.5 0.7 select_select_fusion
  691.2 1.1 scatter.19
  692.2 0.9 and_select_fusion
  (40 shorter events, 6.7 us)
Async XLA Ops:
  6.5 272.9 %all-reduce.3.cloned.1.call-start = ((), (), s32[]{:S(2)}) async-start(), calls=%async_computation.2 | async-start | bytes 262144 | tf_op jit(solution)/shard_map/psum | solution.py:11
  282.0 60.1 %all-to-all-start = ((f32[32,256,64]{1,2,0:T(8,128)}), f32[32,256,64]{1,2,0:T(8,128)S(1)}, u32[]{:S(2)}, u32[]{:S(2)}) async-start(f32[32,256,64]{1,2,0:T(8,128)} %stack.4), calls=%async_computation | async-start | bytes 4194304 | tf_op jit(solution)/shard_map/all_to_all | solution.py:33
  291.9 324.0 %all-reduce.5.cloned.1.call-start = ((), (), s32[]{:S(2)}) async-start(), calls=%async_computation.3 | async-start | bytes 262144 | tf_op jit(solution)/shard_map/psum | solution.py:11
  345.2 8.2 %copy-start = (f32[256,64]{1,0:T(8,128)S(1)}, f32[256,64]{1,0:T(8,128)}, u32[]{:S(2)}) copy-start(f32[256,64]{1,0:T(8,128)} %all-reduce.3.cloned.1.call-done) | copy-start | bytes 196612
  345.2 8.2 %copy-start.2 = (f32[256,512]{1,0:T(8,128)S(1)}, f32[256,512]{1,0:T(8,128)}, u32[]{:S(2)}) copy-start(f32[256,512]{1,0:T(8,128)} %param.14) | copy-start | bytes 1572868
  618.5 60.1 %all-to-all-start.1 = ((f32[32,256,64]{1,2,0:T(8,128)}), f32[32,256,64]{1,2,0:T(8,128)S(1)}, u32[]{:S(2)}, u32[]{:S(2)}) async-start(f32[32,256,64]{1,2,0:T(8,128)} %stack.5), calls=%async_computation.1 | async-start | bytes 4194304 | tf_op jit(solution)/shard_map/all_to_all | solution.py:33
  681.7 8.1 %copy-start.1 = (f32[256,64]{1,0:T(8,128)S(1)}, f32[256,64]{1,0:T(8,128)}, u32[]{:S(2)}) copy-start(f32[256,64]{1,0:T(8,128)} %all-reduce.5.cloned.1.call-done) | copy-start | bytes 196612
Sparse Core Ops, SparseCore 0:
  154.5 124.9 all-reduce.2
  496.3 119.5 all-reduce.4

commit v2 on v0

--- a/solution.py
+++ b/solution.py
@@ -8,7 +8,7 @@
 
 def spread(array, axis, root):
     mine = lax.axis_index(axis) == root
-    return lax.psum(jnp.where(mine, array, jnp.zeros_like(array)), axis)
+    return jnp.sum(lax.all_gather(jnp.where(mine, array, jnp.zeros_like(array)), axis), axis=0)
 
 
 def factor_panel(matrix, panel_index, row_ids, nrows, ncols):

time: 752 us -> 427 us (0.57)
  blocking collectives: 271 us -> 99.7 us
  waiting for transfers between devices: 414 us -> 256 us
    psum x2 -> x0, blocking collectives: 271 us -> none  [spread(): return lax.psum(jnp.where(mine, array, jnp.zeros_like(array)), axis)]
    psum x2 -> x0, waiting for transfers between devices: 235 us -> none  [spread(): return lax.psum(jnp.where(mine, array, jnp.zeros_like(array)), axis)]
    all_gather x0 -> x2, blocking collectives: none -> 99.7 us  [spread(): lax.all_gather(jnp.where(mine, array, jnp.zeros_like(array)), axis)]
    all_gather x0 -> x2, waiting for transfers between devices: none -> 86.1 us  [spread(): lax.all_gather(jnp.where(mine, array, jnp.zeros_like(array)), axis)]
    all_gather x2, waiting for transfers between devices: 178 us -> 170 us  [matching_rows(): gathered = lax.all_gather(panel_block, 'row', axis=0, tiled=True)]
where the time goes in v2:
time: 427 us; the launch traced here: 426 us
  waiting for transfers between devices  256 us (60%)
  blocking collectives  99.7 us (23%)
  other arithmetic  35.5 us (8%)
  local copies, waits for them, and re-layouts  17.9 us (4%)
  between operations  14.6 us (3%)
    all_gather x2, waiting for transfers between devices, matching_rows(): gathered = lax.all_gather(panel_block, 'row', axis=0, tiled=True)  170 us
    all_gather x2, blocking collectives, spread(): lax.all_gather(jnp.where(mine, array, jnp.zeros_like(array)), axis)  99.7 us
    all_gather x2, waiting for transfers between devices, spread(): lax.all_gather(jnp.where(mine, array, jnp.zeros_like(array)), axis)  86.1 us
    another operation x6, other arithmetic, factor_panel(): diag_factor = jnp.linalg.cholesky(corner)  13 us
    another operation x4, other arithmetic, factor_panel(): jax.scipy.linalg.solve_triangular(diag_factor, column_part.T, lower=True)  11.1 us
    reshape x2, local copies, waits for them, and re-layouts, matching_rows(): gathered.reshape(nrows, row_count, NB, NB).transpose(1, 0, 2, 3)  9.59 us
  transfers between devices with their start and end apart: 4, of which 4 were waited for; matrix products, arithmetic and copies ran while one was open for 0% of the time, Pallas kernels for 0%

profile of v2, /device:TPU:8, one launch (start us, length us, event | category | flops | bytes accessed | tf_op | source)
XLA Modules:
  0.0 426.4 jit_solution(13494326304574176114)
XLA Ops:
  6.6 0.8 slice_select_fusion.3
  7.3 52.5 %all-gather = f32[2048,64]{1,0:T(8,128)S(1)} all-gather(f32[64,64]{1,0:T(8,128)S(1)} %slice_select_fusion.3), channel_id=2, replica_groups=mesh['row'=32,'col'=16] {'row'}, dimensions={0}, use_global_device_ids=true | all-gather | bytes 540672 | tf_op jit(solution)/shard_map/all_gather | solution.py:11
  60.0 5.8 %cholesky.44 = f32[64,64]{1,0:T(8,128)S(1)} custom-call(f32[64,64]{1,0:T(8,128)S(1)} %fusion.12), custom_call_target="Cholesky" | custom-call | tf_op jit(solution)/shard_map/jit(cholesky)/cholesky | solution.py:19
  65.9 0.6 compare_reduce_fusion.1
  66.6 0.7 select_bitcast_fusion.1
  67.2 4.9 %custom-call.6 = f32[1,64,64]{1,2,0:T(8,128)S(1)} custom-call(f32[1,64,64]{2,1,0:T(8,128)S(1)} %select_bitcast_fusion.1), custom_call_target="InvertDiagBlocksLowerTriangular" | custom-call | tf_op jit(solution)/shard_map/jit(_solve_triangular)/triangular_solve | solution.py:21
  72.7 1.2 fusion.3
  74.4 0.7 fusion.8
  75.1 0.7 broadcast_select_fusion.3
  75.9 43.3 %all-gather.13.cloned.1.call-done = f32[4096,64]{1,0:T(8,128)} async-done(((f32[256,64]{1,0:T(8,128)}), f32[4096,64]{1,0:T(8,128)}) %all-gather.13.cloned.1.call-update) | async-done | bytes 1048592 | tf_op jit(solution)/shard_map/all_gather | solution.py:11
  119.1 2.4 reduce_sum.37
  122.2 0.6 compare_reduce_fusion.2
  122.9 84.8 %all-gather.9.cloned.1.call-done = f32[8192,64]{1,0:T(8,128)} async-done(((f32[256,64]{1,0:T(8,128)}), f32[8192,64]{1,0:T(8,128)}) %all-gather.9.cloned.1.call-update) | async-done | bytes 2097168 | tf_op jit(solution)/shard_map/all_gather | solution.py:32
  207.7 4.8 %copy.14 = f32[32,4,64,64]{3,2,0,1:T(8,128)} copy(f32[32,4,64,64]{3,2,1,0:T(8,128)} %bitcast.50) | data formatting | bytes 4194304 | tf_op jit(solution)/shard_map/reshape | solution.py:34
  212.5 2.7 gather_fusion
  215.4 0.6 fusion
  216.6 47.1 %all-gather.2 = f32[2048,64]{1,0:T(8,128)S(1)} all-gather(f32[64,64]{1,0:T(8,128)S(1)} %slice_select_fusion.1), channel_id=4, replica_groups=mesh['row'=32,'col'=16] {'row'}, dimensions={0}, use_global_device_ids=true | all-gather | bytes 540672 | tf_op jit(solution)/shard_map/all_gather | solution.py:11
  264.0 5.8 %cholesky.55 = f32[64,64]{1,0:T(8,128)S(1)} custom-call(f32[64,64]{1,0:T(8,128)S(1)} %fusion.10), custom_call_target="Cholesky" | custom-call | tf_op jit(solution)/shard_map/jit(cholesky)/cholesky | solution.py:19
  269.8 0.6 compare_reduce_fusion
  270.5 0.7 select_bitcast_fusion
  271.1 4.9 %custom-call.7 = f32[1,64,64]{1,2,0:T(8,128)S(1)} custom-call(f32[1,64,64]{2,1,0:T(8,128)S(1)} %select_bitcast_fusion), custom_call_target="InvertDiagBlocksLowerTriangular" | custom-call | tf_op jit(solution)/shard_map/jit(_solve_triangular)/triangular_solve | solution.py:21
  276.3 0.7 fusion.7
  277.0 0.7 broadcast_select_fusion.2
  277.7 42.8 %all-gather.15.cloned.1.call-done = f32[4096,64]{1,0:T(8,128)} async-done(((f32[256,64]{1,0:T(8,128)}), f32[4096,64]{1,0:T(8,128)}) %all-gather.15.cloned.1.call-update) | async-done | bytes 1048592 | tf_op jit(solution)/shard_map/all_gather | solution.py:11
  320.5 2.4 reduce_sum.39
  323.0 1.1 scatter.15
  324.1 84.9 %all-gather.11.cloned.1.call-done = f32[8192,64]{1,0:T(8,128)} async-done(((f32[256,64]{1,0:T(8,128)}), f32[8192,64]{1,0:T(8,128)}) %all-gather.11.cloned.1.call-update) | async-done | bytes 2097168 | tf_op jit(solution)/shard_map/all_gather | solution.py:32
  409.0 4.8 %copy.17 = f32[32,4,64,64]{3,2,0,1:T(8,128)} copy(f32[32,4,64,64]{3,2,1,0:T(8,128)} %bitcast.51) | data formatting | bytes 4194304 | tf_op jit(solution)/shard_map/reshape | solution.py:34
  413.8 2.7 gather_fusion.1
  416.6 0.6 fusion.1
  417.9 1.1 scatter.19
  418.9 0.9 and_select_fusion
  (38 shorter events, 2.8 us)
Async XLA Ops:
  6.5 112.6 %all-gather.13.cloned.1.call-start = ((), (), s32[]{:S(2)}) async-start(), calls=%async_computation.2 | async-start | bytes 2228224 | tf_op jit(solution)/shard_map/all_gather | solution.py:11
  75.8 131.9 %all-gather.9.cloned.1.call-start = ((), (), s32[]{:S(2)}) async-start(), calls=%async_computation | async-start | bytes 4325376 | tf_op jit(solution)/shard_map/all_gather | solution.py:32
  121.5 199.0 %all-gather.15.cloned.1.call-start = ((), (), s32[]{:S(2)}) async-start(), calls=%async_computation.3 | async-start | bytes 2228224 | tf_op jit(solution)/shard_map/all_gather | solution.py:11
  207.7 7.7 %copy-start = (f32[256,64]{1,0:T(8,128)S(1)}, f32[256,64]{1,0:T(8,128)}, u32[]{:S(2)}) copy-start(f32[256,64]{1,0:T(8,128)} %reduce_sum.37) | copy-start | bytes 196612
  207.7 7.7 %copy-start.2 = (f32[256,512]{1,0:T(8,128)S(1)}, f32[256,512]{1,0:T(8,128)}, u32[]{:S(2)}) copy-start(f32[256,512]{1,0:T(8,128)} %param.14) | copy-start | bytes 1572868
  277.7 131.3 %all-gather.11.cloned.1.call-start = ((), (), s32[]{:S(2)}) async-start(), calls=%async_computation.1 | async-start | bytes 4325376 | tf_op jit(solution)/shard_map/all_gather | solution.py:32
  409.0 7.6 %copy-start.1 = (f32[256,64]{1,0:T(8,128)S(1)}, f32[256,64]{1,0:T(8,128)}, u32[]{:S(2)}) copy-start(f32[256,64]{1,0:T(8,128)} %reduce_sum.39) | copy-start | bytes 196612
Sparse Core Ops, SparseCore 0:
  75.9 43.1 all-gather.12
  122.3 85.3 all-gather.8
  277.8 42.7 all-gather.14
  323.6 85.3 all-gather.10
